TPU v7x, 128 devices: a whole 4x4x4 slice. The times are simulated.
128 devices in a mesh: chaos: 8 (over x, y_hi), space: 16 (over y_lo, z, core).
Axes of the slice: x: 4, y: 4 (y_hi: 2, y_lo: 2; y = y_hi * 2 + y_lo), z: 4, core: 2. Of those that a mesh axis runs over, the one named last changes fastest.
Arguments:
- modes: float32 [120, 128, 2048], P('chaos', 'space'), may hold values from -2 to 2
- kl_fields: float32 [8, 128, 2048], P(None, 'space'), may hold values from 0.1 to 1
- triples: int32 [624, 3], replicated, may hold values from 0 to 119, as said below
- ratios: int32 [624, 2], replicated, may hold values from 1 to 12, as said below
- mode_of_slot: int32 [120], replicated, may hold values from 0 to 119, each once
Outputs:
- applied: float32 [120, 128, 2048], P('chaos', 'space')
Inputs may be any that keep to these rules, and one draw needn't show every extreme that they name: `triples`: rows are distinct. Modes are the multi-indices of total degree at most 3 in 7 variables. Every mode i has the row (i, i, 0); every other row (i, j, k) has k of 1 or more, and the multi-indices of i and j differ by one in variable k and agree elsewhere; each such pair appears in both orders. `ratios`: column 0 is a positive numerator, column 1 a denominator of 1 to 4. `mode_of_slot`: A permutation.
All inputs are finite; a program needn't handle non-finite values.
Results may differ from a plain program's by a relative error of at most 0.000082.
Values sent between devices are 32-bit elements; how exact they have to be, the bound alone decides.
No kernel may reach another device: no remote copies, remote signals or barrier semaphores. Data moves between devices by JAX's collectives and lax.ppermute only.
A program may use at most 128 MiB of HBM per device.

v0:
```python
import jax
import jax.numpy as jnp
from jax import lax
from jax.sharding import PartitionSpec as P

HIGHEST_PRECISION = lax.Precision.HIGHEST


def extended_2(x, sides, width):
    for axis, dim in sides:
        count, length = (lax.axis_size(axis), x.shape[dim])
        up = [(i, (i + 1) % count) for i in range(count - 1)]
        down = [(j, i) for i, j in up]
        last = lax.slice_in_dim(x, length - width, length, axis=dim)
        first = lax.slice_in_dim(x, 0, width, axis=dim)
        before = lax.ppermute(last, axis, up)
        after = lax.ppermute(first, axis, down)
        x = jnp.concatenate([before, x, after], axis=dim)
    return x


def from_root(block, axis, owner):
    block = jnp.where(lax.axis_index(axis) == owner, block, jnp.zeros_like(block))
    return lax.psum(block, axis)


def diffuse(values, factor):
    center = values[:, 1:-1, :]
    coef_mid = factor[1:-1, :]
    result = (coef_mid + factor[:-2, :]) * (center - values[:, :-2, :])
    result = result + (coef_mid + factor[2:, :]) * (center - values[:, 2:, :])
    zero_col = jnp.zeros_like(center[:, :, :1])
    left_cell = jnp.concatenate([zero_col, center[:, :, :-1]], axis=2)
    right_cell = jnp.concatenate([center[:, :, 1:], zero_col], axis=2)
    coef_zero = jnp.zeros_like(coef_mid[:, :1])
    coef_left = jnp.concatenate([coef_zero, coef_mid[:, :-1]], axis=1)
    coef_right = jnp.concatenate([coef_mid[:, 1:], coef_zero], axis=1)
    result = result + (coef_mid + coef_left) * (center - left_cell)
    result = result + (coef_mid + coef_right) * (center - right_cell)
    return 0.5 * result


def coupling_table(triples, ratios, mode_of_slot, kl_terms, mode_count):
    matches = triples[:, :2, None] == mode_of_slot[None, None, :]
    slot_pairs = jnp.sum(jnp.where(matches, jnp.arange(mode_count, dtype=jnp.int32), 0), axis=2)
    weights = ratios[:, 0].astype(jnp.float32) / ratios[:, 1].astype(jnp.float32)
    flat_index = (triples[:, 2] * mode_count + slot_pairs[:, 0]) * mode_count + slot_pairs[:, 1]
    coupling = (
        jnp.zeros((kl_terms * mode_count * mode_count,), jnp.float32).at[flat_index].add(weights)
    )
    return coupling.reshape(kl_terms, mode_count, mode_count)


def local(modes, kl_fields, triples, ratios, mode_of_slot):
    groups = lax.axis_size("chaos")
    own_modes = modes.shape[0]
    mode_count = own_modes * groups
    kl_terms = kl_fields.shape[0]
    slab_rows = modes.shape[1]
    raster_cols = modes.shape[2]
    first_slot = lax.axis_index("chaos") * own_modes
    coupling = coupling_table(triples, ratios, mode_of_slot, kl_terms, mode_count)
    local_rows = lax.dynamic_slice_in_dim(coupling, first_slot, own_modes, 1).reshape(
        kl_terms * own_modes, mode_count
    )
    joined = jnp.concatenate([modes, kl_fields], axis=0)
    padded = extended_2(joined, (("space", 1),), 1)
    source = padded[:own_modes]
    coefficients = padded[own_modes:]
    rim_depth = source.shape[1]
    flat_source = source.reshape(own_modes, rim_depth * raster_cols)
    zero_sum = jnp.zeros((kl_terms * own_modes, rim_depth * raster_cols), jnp.float32)
    mixed_fields = zero_sum
    for owner in range(groups):
        received = from_root(flat_source, "chaos", owner)
        mode_block = lax.dynamic_slice_in_dim(local_rows, owner * own_modes, received.shape[0], 1)
        mixed_fields = mixed_fields + jnp.dot(
            mode_block, received, precision=HIGHEST_PRECISION, preferred_element_type=jnp.float32
        )
    extended = mixed_fields.reshape(kl_terms, own_modes, rim_depth, raster_cols)
    applied = jnp.zeros((own_modes, slab_rows, raster_cols), jnp.float32)
    for kl_index in range(kl_terms):
        applied = applied + diffuse(extended[kl_index], coefficients[kl_index])
    return applied


def solution(mesh):
    return jax.shard_map(
        local,
        mesh=mesh,
        in_specs=(P("chaos", "space", None), P(None, "space", None), P(), P(), P()),
        out_specs=P("chaos", "space", None),
        check_vma=False,
    )
```

profile of v0, /device:TPU:5, one launch (start us, length us, event | category | flops | bytes accessed | tf_op | source)
XLA Modules:
  0.0 603.4 jit_solution(7292626513668426113)
XLA Ops:
  8.2 2.6 collective-permute-start.1
  10.9 3.4 collective-permute-start
  18.4 1.8 copy.47
  20.5 1.8 copy.40
  22.5 1.9 copy.41
  24.7 1.8 copy.42
  27.8 1.8 copy.46
  29.8 1.9 copy.43
  31.9 1.8 copy.44
  34.0 1.9 copy.45
  36.8 4.9 scatter_custom_fusion
  46.8 419.7 %all-reduce.35.cloned.1.call-done = (f32[15,20480]{1,0:T(8,128)}, f32[15,20480]{1,0:T(8,128)}, f32[15,20480]{1,0:T(8,128)}, f32[15,20480]{1,0:T(8,128)}, f32[15,...) async-done(((f32[15,20480]{1,0:T(8,128)}, f32[15,20480]{1,0:T(8,128)}, f32[15,20480]{1,0:T(8,128)}, f32[15,20480]{1,0:T(8,128)}, ...) | async-done | bytes 9830416 | tf_op jit(solution)/shard_map/psum | solution.py:24
  466.5 9.2 %fusion.75 = f32[120,20480]{1,0:T(8,128)S(1)} fusion(f32[15,20480]{1,0:T(8,128)} %get-tuple-element.5, f32[120,120]{1,0:T(8,128)S(1)} %reshape.94), kind=kOutput, calls=%fused_computation.142 | convolution fusion | flops 442368000 | bytes 11116800 | tf_op jit(solution)/shard_map/dot_general | solution.py:77
  475.8 8.2 %convolution_add_fusion.6 = f32[120,20480]{1,0:T(8,128)S(1)} fusion(f32[120,20480]{1,0:T(8,128)S(1)} %fusion.75, f32[15,20480]{1,0:T(8,128)S(1)} %copy-done.13, f32[120,120]{1,0:T(8,128)S(1)} %reshape.94), kind=kOutput, calls=%fused_computation.7 | convolution fusion | flops 444825600 | bytes 20947200 | tf_op jit(solution)/shard_map/dot_general | solution.py:77
  484.0 8.3 %convolution_add_fusion.5 = f32[120,20480]{1,0:T(8,128)S(1)} fusion(f32[120,20480]{1,0:T(8,128)S(1)} %convolution_add_fusion.6, f32[15,20480]{1,0:T(8,128)S(1)} %copy-done.12, f32[120,120]{1,0:T(8,128)S(1)} %reshape.94), kind=kOutput, calls=%fused_computation.6 | convolution fusion | flops 444825600 | bytes 20947200 | tf_op jit(solution)/shard_map/dot_general | solution.py:77
  492.3 7.9 %convolution_add_fusion.4 = f32[120,20480]{1,0:T(8,128)S(1)} fusion(f32[120,20480]{1,0:T(8,128)S(1)} %convolution_add_fusion.5, f32[15,20480]{1,0:T(8,128)S(1)} %copy-done.11, f32[120,120]{1,0:T(8,128)S(1)} %reshape.94), kind=kOutput, calls=%fused_computation.5 | convolution fusion | flops 444825600 | bytes 20947200 | tf_op jit(solution)/shard_map/dot_general | solution.py:77
  500.3 8.1 %convolution_add_fusion.3 = f32[120,20480]{1,0:T(8,128)S(1)} fusion(f32[120,20480]{1,0:T(8,128)S(1)} %convolution_add_fusion.4, f32[15,20480]{1,0:T(8,128)S(1)} %copy-done.10, f32[120,120]{1,0:T(8,128)S(1)} %reshape.94), kind=kOutput, calls=%fused_computation.4 | convolution fusion | flops 444825600 | bytes 20947200 | tf_op jit(solution)/shard_map/dot_general | solution.py:77
  508.4 7.9 %convolution_add_fusion.2 = f32[120,20480]{1,0:T(8,128)S(1)} fusion(f32[120,20480]{1,0:T(8,128)S(1)} %convolution_add_fusion.3, f32[15,20480]{1,0:T(8,128)S(1)} %copy-done.9, f32[120,120]{1,0:T(8,128)S(1)} %reshape.94), kind=kOutput, calls=%fused_computation.3 | convolution fusion | flops 444825600 | bytes 20947200 | tf_op jit(solution)/shard_map/dot_general | solution.py:77
  516.4 10.0 %convolution_add_fusion.1 = f32[120,20480]{1,0:T(8,128)S(1)} fusion(f32[120,20480]{1,0:T(8,128)S(1)} %convolution_add_fusion.2, f32[15,20480]{1,0:T(8,128)S(1)} %copy-done.8, f32[120,120]{1,0:T(8,128)S(1)} %reshape.94), kind=kOutput, calls=%fused_computation.2 | convolution fusion | flops 444825600 | bytes 20947200 | tf_op jit(solution)/shard_map/dot_general | solution.py:77
  526.4 10.8 %convolution_add_fusion = f32[120,20480]{1,0:T(8,128)} fusion(f32[120,20480]{1,0:T(8,128)S(1)} %convolution_add_fusion.1, f32[15,20480]{1,0:T(8,128)S(1)} %copy-done.7, f32[120,120]{1,0:T(8,128)S(1)} %reshape.94), kind=kOutput, calls=%fused_computation.1 | convolution fusion | flops 444825600 | bytes 20947200 | tf_op jit(solution)/shard_map/dot_general | solution.py:77
  537.1 8.7 %fusion.80 = (f32[15,20480]{1,0:T(8,128)}, f32[15,20480]{1,0:T(8,128)}, f32[15,20480]{1,0:T(8,128)}, f32[15,20480]{1,0:T(8,128)}, f32[15,20480]{1,0:T(8,128)}, /...) fusion(f32[120,20480]{1,0:T(8,128)} %convolution_add_fusion), kind=kLoop, calls=%fused_computation.162 | loop fusion | bytes 19660800 | tf_op jit(solution)/shard_map/slice | solution.py:83
  547.6 3.1 squeeze.44
  550.7 3.1 squeeze.43
  553.8 3.0 squeeze.42
  556.8 3.1 squeeze.20
  559.9 3.1 squeeze.19
  563.0 3.0 squeeze.18
  567.8 4.2 fusion.81
  572.0 2.6 fusion.83
  575.4 2.6 fusion.85
  579.0 2.6 fusion.87
  581.7 14.4 %fusion.5 = f32[15,8,2048]{2,1,0:T(8,128)} fusion(f32[15,10,2048]{2,1,0:T(8,128)S(1)} %copy-done, f32[15,10,2048]{2,1,0:T(8,128)S(1)} %copy-done.1, f32[15,10,2048]{2,1,0:T(8,128)S(1)} %copy-done.2, f32[15,10,2048]{2,1,0:T(8,128)S(1)} %copy-done.3, f32[15,10,2048]{2,1,0:T(8,128)} %squeeze.19, f32[15,10,2048]{2,1,0:T(8,128)} %squeeze.18, ...), kind=kLoop, calls=%fused_computation.16 | loop fusion | flops 23592960 | bytes 42394112 | tf_op jit(solution)/shard_map/add | solution.py:83
  (104 shorter events, 19.7 us)
Async XLA Ops:
  6.5 1.3 copy-start.6
  6.5 460.0 %all-reduce.35.cloned.1.call-start = ((), (), s32[]{:S(2)}) async-start(), calls=%async_computation | async-start | bytes 20971520 | tf_op jit(solution)/shard_map/psum | solution.py:24
  8.2 7.5 %collective-permute-start.1 = (f32[23,1,2048]{2,0,1:T(8,128)S(1)}, f32[23,1,2048]{2,0,1:T(8,128)S(1)}, u32[]{:S(2)}, u32[]{:S(2)}) collective-permute-start(f32[23,1,2048]{2,0,1:T(8,128)S(1)} %copy.36), channel_id=1, source_target_pairs={{1,0},{2,1},{3,2},{4,3},{5,4},{6,5},{7,6},{8,7},{9,8},{10,9},{11,1... | collective-permute-start | bytes 565256 | tf_op jit(solution)/shard_map/ppermute | solution.py:17
  10.9 6.0 %collective-permute-start = (f32[23,1,2048]{2,0,1:T(8,128)S(1)}, f32[23,1,2048]{2,0,1:T(8,128)S(1)}, u32[]{:S(2)}, u32[]{:S(2)}) collective-permute-start(f32[23,1,2048]{2,0,1:T(8,128)S(1)} %copy.34), channel_id=1, source_target_pairs={{0,1},{1,2},{2,3},{3,4},{4,5},{5,6},{6,7},{7,8},{8,9},{9,10},{10,1... | collective-permute-start | bytes 565256 | tf_op jit(solution)/shard_map/ppermute | solution.py:16
  466.5 9.3 %copy-start.13 = (f32[15,20480]{1,0:T(8,128)S(1)}, f32[15,20480]{1,0:T(8,128)}, u32[]{:S(2)}) copy-start(f32[15,20480]{1,0:T(8,128)} %get-tuple-element.6) | copy-start | bytes 3686404
  475.8 8.2 %copy-start.12 = (f32[15,20480]{1,0:T(8,128)S(1)}, f32[15,20480]{1,0:T(8,128)}, u32[]{:S(2)}) copy-start(f32[15,20480]{1,0:T(8,128)} %get-tuple-element.7) | copy-start | bytes 3686404
  483.9 8.4 %copy-start.11 = (f32[15,20480]{1,0:T(8,128)S(1)}, f32[15,20480]{1,0:T(8,128)}, u32[]{:S(2)}) copy-start(f32[15,20480]{1,0:T(8,128)} %get-tuple-element.8) | copy-start | bytes 3686404
  492.3 7.9 %copy-start.10 = (f32[15,20480]{1,0:T(8,128)S(1)}, f32[15,20480]{1,0:T(8,128)}, u32[]{:S(2)}) copy-start(f32[15,20480]{1,0:T(8,128)} %get-tuple-element.9) | copy-start | bytes 3686404
  500.3 8.1 %copy-start.9 = (f32[15,20480]{1,0:T(8,128)S(1)}, f32[15,20480]{1,0:T(8,128)}, u32[]{:S(2)}) copy-start(f32[15,20480]{1,0:T(8,128)} %get-tuple-element.10) | copy-start | bytes 3686404
  508.4 7.9 %copy-start.8 = (f32[15,20480]{1,0:T(8,128)S(1)}, f32[15,20480]{1,0:T(8,128)}, u32[]{:S(2)}) copy-start(f32[15,20480]{1,0:T(8,128)} %get-tuple-element.11) | copy-start | bytes 3686404
  516.4 10.0 %copy-start.7 = (f32[15,20480]{1,0:T(8,128)S(1)}, f32[15,20480]{1,0:T(8,128)}, u32[]{:S(2)}) copy-start(f32[15,20480]{1,0:T(8,128)} %get-tuple-element.12) | copy-start | bytes 3686404
  567.8 4.2 copy-start.4
  567.8 4.2 copy-start.5
  572.0 2.6 copy-start.2
  572.0 3.5 copy-start.3
  575.4 2.6 copy-start
  575.4 3.5 copy-start.1
  578.9 2.7 copy-start.14
  578.9 2.7 copy-start.15
  578.9 2.7 copy-start.16
  578.9 2.7 copy-start.17
  578.9 2.7 copy-start.18
  578.9 2.7 copy-start.19
  578.9 2.7 copy-start.20
  579.0 2.7 copy-start.21
  579.0 2.7 copy-start.22
  579.0 2.7 copy-start.23
  579.0 2.7 copy-start.24
  579.0 2.7 copy-start.25
  579.0 2.7 copy-start.26
  579.0 2.7 copy-start.27
  579.0 2.7 copy-start.28
  (4 other events, 3.1 us)
Sparse Core Ops, SparseCore 0:
  36.0 430.4 all-reduce.34
where the time goes:
time: 612 us; the launch traced here: 603 us
  waiting for transfers between devices  422 us (69%)
  matrix products  70.4 us (12%)
  local copies, waits for them, and re-layouts  64.6 us (11%)
  other arithmetic  25.7 us (4%)
  between operations  14.4 us (2%)
    psum x1, waiting for transfers between devices, from_root(): return lax.psum(block, axis)  420 us
    dot_general x8, matrix products, local(): jnp.dot(mode_block, received, precision=HIGHEST_PRECISION, preferred_elem...  70.4 us
    squeeze x8, local copies, waits for them, and re-layouts, local(): applied = applied + diffuse(extended[kl_index], coefficients[kl_index])  21.9 us
    unnamed x81, local copies, waits for them, and re-layouts  19.7 us
    add x1, other arithmetic, local(): applied = applied + diffuse(extended[kl_index], coefficients[kl_index])  14.4 us
  transfers between devices with their start and end apart: 3, of which 3 were waited for; matrix products, arithmetic and copies ran while one was open for 2% of the time, Pallas kernels for 0%

commit v1 on v0

--- a/solution.py
+++ b/solution.py
@@ -21,7 +21,7 @@
 
 def from_root(block, axis, owner):
     block = jnp.where(lax.axis_index(axis) == owner, block, jnp.zeros_like(block))
-    return lax.psum(block, axis)
+    return jnp.sum(lax.all_gather(block, axis), axis=0)
 
 
 def diffuse(values, factor):

time: 612 us -> 1140 us (1.86)
  waiting for transfers between devices: 422 us -> 891 us
  other arithmetic: 25.7 us -> 74.6 us
    all_gather x0 -> x8, waiting for transfers between devices: none -> 888 us  [from_root(): return jnp.sum(lax.all_gather(block, axis), axis=0)]
    psum x1 -> x0, waiting for transfers between devices: 420 us -> none  [from_root(): return lax.psum(block, axis)]
    reduce_sum x0 -> x8, other arithmetic: none -> 43.4 us  [from_root(): return jnp.sum(lax.all_gather(block, axis), axis=0)]
    select_n x0 -> x8, local copies, waits for them, and re-layouts: none -> 25.4 us  [from_root(): jnp.where(lax.axis_index(axis) == owner, block, jnp.zeros_like(block))]
    unnamed x81 -> x59, local copies, waits for them, and re-layouts: 19.7 us -> 3.19 us
  transfers between devices with their start and end apart: 3 -> 10, of which waited for: 3 -> 10; matrix products, arithmetic and copies ran while one was open for 2% -> 12% of each run, Pallas kernels for 0% -> 0%
where the time goes in v1:
time: 1140 us; the launch traced here: 1130 us
  waiting for transfers between devices  891 us (78%)
  other arithmetic  74.6 us (7%)
  matrix products  73.2 us (6%)
  local copies, waits for them, and re-layouts  72.9 us (6%)
  between operations  14.5 us (1%)
    all_gather x8, waiting for transfers between devices, from_root(): return jnp.sum(lax.all_gather(block, axis), axis=0)  888 us
    dot_general x8, matrix products, local(): jnp.dot(mode_block, received, precision=HIGHEST_PRECISION, preferred_elem...  73.2 us
    reduce_sum x8, other arithmetic, from_root(): return jnp.sum(lax.all_gather(block, axis), axis=0)  43.4 us
    select_n x8, local copies, waits for them, and re-layouts, from_root(): jnp.where(lax.axis_index(axis) == owner, block, jnp.zeros_like(block))  25.4 us
  transfers between devices with their start and end apart: 10, of which 10 were waited for; matrix products, arithmetic and copies ran while one was open for 12% of the time, Pallas kernels for 0%

profile of v1, /device:TPU:5, one launch (start us, length us, event | category | flops | bytes accessed | tf_op | source)
XLA Modules:
  0.0 1132.6 jit_solution(17266581427809191896)
XLA Ops:
  10.9 3.4 collective-permute-start
  17.1 3.7 broadcast_select_fusion
  30.5 3.7 broadcast_select_fusion.1
  40.7 3.4 select_n.158
  50.9 4.9 scatter_custom_fusion
  60.9 93.4 %all-gather.9.cloned.1.call-done = f32[8,15,20480]{2,1,0:T(8,128)} async-done(((f32[1,15,20480]{2,1,0:T(8,128)}), f32[8,15,20480]{2,1,0:T(8,128)}) %all-gather.9.cloned.1.call-update) | async-done | bytes 9830416 | tf_op jit(solution)/shard_map/all_gather | solution.py:24
  154.3 5.9 reduce_sum.82
  160.2 122.0 %all-gather.11.cloned.1.call-done = f32[8,15,20480]{2,1,0:T(8,128)} async-done(((f32[1,15,20480]{2,1,0:T(8,128)}), f32[8,15,20480]{2,1,0:T(8,128)}) %all-gather.11.cloned.1.call-update) | async-done | bytes 9830416 | tf_op jit(solution)/shard_map/all_gather | solution.py:24
  282.1 4.8 reduce_sum.83
  286.9 123.1 %all-gather.13.cloned.1.call-done = f32[8,15,20480]{2,1,0:T(8,128)} async-done(((f32[1,15,20480]{2,1,0:T(8,128)}), f32[8,15,20480]{2,1,0:T(8,128)}) %all-gather.13.cloned.1.call-update) | async-done | bytes 9830416 | tf_op jit(solution)/shard_map/all_gather | solution.py:24
  410.0 5.8 reduce_sum.84
  415.9 121.9 %all-gather.21.cloned.1.call-done = f32[8,15,20480]{2,1,0:T(8,128)} async-done(((f32[1,15,20480]{2,1,0:T(8,128)}), f32[8,15,20480]{2,1,0:T(8,128)}) %all-gather.21.cloned.1.call-update) | async-done | bytes 9830416 | tf_op jit(solution)/shard_map/all_gather | solution.py:24
  537.7 4.8 reduce_sum.88
  542.5 122.9 %all-gather.15.cloned.1.call-done = f32[8,15,20480]{2,1,0:T(8,128)} async-done(((f32[1,15,20480]{2,1,0:T(8,128)}), f32[8,15,20480]{2,1,0:T(8,128)}) %all-gather.15.cloned.1.call-update) | async-done | bytes 9830416 | tf_op jit(solution)/shard_map/all_gather | solution.py:24
  665.4 5.8 reduce_sum.85
  671.2 121.9 %all-gather.17.cloned.1.call-done = f32[8,15,20480]{2,1,0:T(8,128)} async-done(((f32[1,15,20480]{2,1,0:T(8,128)}), f32[8,15,20480]{2,1,0:T(8,128)}) %all-gather.17.cloned.1.call-update) | async-done | bytes 9830416 | tf_op jit(solution)/shard_map/all_gather | solution.py:24
  793.1 5.8 reduce_sum.86
  798.9 122.0 %all-gather.19.cloned.1.call-done = f32[8,15,20480]{2,1,0:T(8,128)} async-done(((f32[1,15,20480]{2,1,0:T(8,128)}), f32[8,15,20480]{2,1,0:T(8,128)}) %all-gather.19.cloned.1.call-update) | async-done | bytes 9830416 | tf_op jit(solution)/shard_map/all_gather | solution.py:24
  921.0 5.8 reduce_sum.87
  926.8 9.4 fusion.75
  936.2 7.9 convolution_add_fusion.6
  944.1 8.4 convolution_add_fusion.5
  952.5 8.1 convolution_add_fusion.4
  960.6 7.9 convolution_add_fusion.3
  968.6 8.2 convolution_add_fusion.2
  976.7 10.8 convolution_add_fusion.1
  987.6 61.3 %all-gather.23.cloned.1.call-done = f32[8,15,20480]{2,1,0:T(8,128)} async-done(((f32[1,15,20480]{2,1,0:T(8,128)}), f32[8,15,20480]{2,1,0:T(8,128)}) %all-gather.23.cloned.1.call-update) | async-done | bytes 9830416 | tf_op jit(solution)/shard_map/all_gather | solution.py:24
  1048.8 4.8 reduce_sum.89
  1053.6 12.6 %convolution_add_fusion = f32[120,20480]{1,0:T(8,128)} fusion(f32[120,20480]{1,0:T(8,128)} %convolution_add_fusion.1, f32[15,20480]{1,0:T(8,128)S(1)} %reduce_sum.89, f32[120,120]{1,0:T(8,128)S(1)} %reshape.174), kind=kOutput, calls=%fused_computation.1 | convolution fusion | flops 444825600 | bytes 20947200 | tf_op jit(solution)/shard_map/dot_general | solution.py:77
  1066.2 8.8 fusion.80
  1096.9 4.2 fusion.81
  1110.8 14.5 %fusion.5 = f32[15,8,2048]{2,1,0:T(8,128)} fusion(f32[15,10,2048]{2,1,0:T(8,128)S(1)} %copy-done, f32[15,10,2048]{2,1,0:T(8,128)S(1)} %copy-done.1, f32[15,10,2048]{2,1,0:T(8,128)S(1)} %copy-done.2, f32[15,10,2048]{2,1,0:T(8,128)S(1)} %copy-done.3, f32[15,10,2048]{2,1,0:T(8,128)} %squeeze.19, f32[15,10,2048]{2,1,0:T(8,128)} %squeeze.18, ...), kind=kLoop, calls=%fused_computation.16 | loop fusion | flops 23592960 | bytes 42394112 | tf_op jit(solution)/shard_map/add | solution.py:83
  (119 shorter events, 66.4 us)
Async XLA Ops:
  6.5 147.8 %all-gather.9.cloned.1.call-start = ((), (), s32[]{:S(2)}) async-start(), calls=%async_computation | async-start | bytes 11796480 | tf_op jit(solution)/shard_map/all_gather | solution.py:24
  8.2 7.5 collective-permute-start.1
  10.9 6.0 collective-permute-start
  24.0 258.1 %all-gather.11.cloned.1.call-start = ((), (), s32[]{:S(2)}) async-start(), calls=%async_computation.1 | async-start | bytes 11796480 | tf_op jit(solution)/shard_map/all_gather | solution.py:24
  27.2 382.8 %all-gather.13.cloned.1.call-start = ((), (), s32[]{:S(2)}) async-start(), calls=%async_computation.2 | async-start | bytes 11796480 | tf_op jit(solution)/shard_map/all_gather | solution.py:24
  30.4 507.3 %all-gather.21.cloned.1.call-start = ((), (), s32[]{:S(2)}) async-start(), calls=%async_computation.6 | async-start | bytes 11796480 | tf_op jit(solution)/shard_map/all_gather | solution.py:24
  37.3 628.1 %all-gather.15.cloned.1.call-start = ((), (), s32[]{:S(2)}) async-start(), calls=%async_computation.3 | async-start | bytes 11796480 | tf_op jit(solution)/shard_map/all_gather | solution.py:24
  40.7 752.4 %all-gather.17.cloned.1.call-start = ((), (), s32[]{:S(2)}) async-start(), calls=%async_computation.4 | async-start | bytes 11796480 | tf_op jit(solution)/shard_map/all_gather | solution.py:24
  44.2 876.8 %all-gather.19.cloned.1.call-start = ((), (), s32[]{:S(2)}) async-start(), calls=%async_computation.5 | async-start | bytes 11796480 | tf_op jit(solution)/shard_map/all_gather | solution.py:24
  47.4 1001.5 %all-gather.23.cloned.1.call-start = ((), (), s32[]{:S(2)}) async-start(), calls=%async_computation.7 | async-start | bytes 11796480 | tf_op jit(solution)/shard_map/all_gather | solution.py:24
  47.4 3.2 slice-start
  47.4 3.2 copy-start.28
  47.4 3.3 copy-start.26
  47.5 3.4 copy-start.27
  936.2 7.9 copy-start.7
  944.1 8.4 copy-start.8
  952.5 8.1 copy-start.9
  960.6 7.9 copy-start.10
  1096.9 4.2 copy-start.4
  1096.9 4.2 copy-start.5
  1101.1 3.5 copy-start.3
  1104.5 3.5 copy-start.1
  1108.0 2.7 copy-start.15
  1108.0 2.7 copy-start.16
  1108.0 2.7 copy-start.17
  1108.0 2.7 copy-start.18
  1108.1 2.7 copy-start.19
  1108.1 2.7 copy-start.20
  1108.1 2.7 copy-start.21
  1108.1 2.7 copy-start.22
  1108.1 2.7 copy-start.23
  1108.1 2.7 copy-start.24
  (8 other events, 19.9 us)
Sparse Core Ops, SparseCore 0:
  24.2 130.0 all-gather.8
  156.6 125.4 all-gather.10
  284.5 125.4 all-gather.12
  412.2 125.4 all-gather.20
  539.9 125.4 all-gather.14
  667.6 125.4 all-gather.16
  795.4 125.4 all-gather.18
  923.3 125.5 all-gather.22
